TPU v7x, 32 devices: a whole 2x2x4 slice. The times are simulated.
32 devices in a mesh: shard: 4 (over z), ctx: 4 (over y, x), tp: 2 (over core).
Axes of the slice: x: 2, y: 2, z: 4, core: 2. Of those that a mesh axis runs over, the one named last changes fastest.
Arguments:
- hidden_in: bfloat16 [24, 680, 1024], P('shard', 'ctx'), may hold values from -6 to 6
- cond: bfloat16 [24, 1024], P('shard'), may hold values from -6 to 6
- scale_len: int32 [24, 10], P('shard'), may hold values from 1 to 256, 680 in all within a row
- ada_weight: bfloat16 [1024, 6, 1024], P('shard'), may hold values from -0.1875 to 0.1875
- ada_bias: float32 [6, 1024], replicated, may hold values from -3 to 3
- qkv_weight: bfloat16 [1024, 3, 1024], P('shard', None, 'tp'), may hold values from -0.1875 to 0.1875
- query_bias: float32 [1024], P('tp'), may hold values from -3 to 3
- value_bias: float32 [1024], P('tp'), may hold values from -3 to 3
- head_scale: float32 [16], P('tp'), may hold values from 2 to 3
- proj_weight: bfloat16 [1024, 1024], P('tp', 'shard'), may hold values from -0.5 to 0.5
- proj_bias: float32 [1024], replicated, may hold values from -2 to 2
- up_weight: bfloat16 [1024, 4096], P('shard', 'tp'), may hold values from -0.1875 to 0.1875
- up_bias: float32 [4096], P('tp'), may hold values from -3 to 3
- down_weight: bfloat16 [4096, 1024], P('tp', 'shard'), may hold values from -0.125 to 0.125
- down_bias: float32 [1024], replicated, may hold values from -2 to 2
- out_grad: bfloat16 [24, 680, 1024], P('shard', 'ctx'), may hold values from -6 to 6
Outputs:
- hidden_out: bfloat16 [24, 680, 1024], P('shard', 'ctx')
- grad_hidden: bfloat16 [24, 680, 1024], P('shard', 'ctx')
- grad_cond: float32 [24, 1024], P('shard')
- grad_ada_weight: float32 [1024, 6, 1024], P('shard')
- grad_ada_bias: float32 [6, 1024], replicated
- grad_qkv_weight: float32 [1024, 3, 1024], P('shard', None, 'tp')
- grad_query_bias: float32 [1024], P('tp')
- grad_value_bias: float32 [1024], P('tp')
- grad_head_scale: float32 [16], P('tp')
- grad_proj_weight: float32 [1024, 1024], P('tp', 'shard')
- grad_proj_bias: float32 [1024], replicated
- grad_up_weight: float32 [1024, 4096], P('shard', 'tp')
- grad_up_bias: float32 [4096], P('tp')
- grad_down_weight: float32 [4096, 1024], P('tp', 'shard')
- grad_down_bias: float32 [1024], replicated
- norm_stats: float32 [3], replicated
Inputs may be any that keep to these rules, and one draw needn't show every extreme that they name: `scale_len`: each row holds the token counts of one map's 10 scales in order; they sum to 680, and the largest in every row is 256.
All inputs are finite; a program needn't handle non-finite values.
Results may differ from a plain program's by a relative error of at most 0.03.
Values may be sent and summed in bfloat16 or wider, within the bound.
No kernel may reach another device: no remote copies, remote signals or barrier semaphores. Data moves between devices by JAX's collectives and lax.ppermute only.
A program may use at most 256 MiB of HBM per device.

v0:
```python
import jax
import jax.numpy as jnp
from jax import lax
from jax.sharding import PartitionSpec as P


def layer_norm(values):
    center = values - jnp.mean(values, axis=-1, keepdims=True)
    spread = jnp.mean(center * center, axis=-1, keepdims=True)
    return center * lax.rsqrt(spread + 1e-06)


def modulate(values, scale, shift):
    return layer_norm(values) * (1.0 + scale[:, None, :]) + shift[:, None, :]


def unit_scaled(values, gains):
    normed = values * lax.rsqrt(jnp.sum(values * values, axis=-1, keepdims=True) + 1e-06)
    return normed * jnp.exp(gains)[None, None, :, None]


def unit_plain(values):
    return values * lax.rsqrt(jnp.sum(values * values, axis=-1, keepdims=True) + 1e-06)


def gelu_tanh(values):
    return jax.nn.gelu(values, approximate=True)


def tp_sum(values):
    count = lax.axis_size("tp")
    if count != 2:
        return lax.psum(values, "tp")
    return values + lax.ppermute(values, "tp", [(0, 1), (1, 0)])


def ctx_shifts(values):
    count = lax.axis_size("ctx")
    parts = [values]
    for shift in range(1, count):
        pairs = [(i, (i + shift) % count) for i in range(count)]
        parts.append(lax.ppermute(values, "ctx", pairs))
    return jnp.stack(parts)


def ctx_return(parts):
    count = lax.axis_size("ctx")
    total = parts[0].astype(jnp.float32)
    for shift in range(1, count):
        pairs = [(i, (i - shift) % count) for i in range(count)]
        total = total + lax.ppermute(parts[shift], "ctx", pairs).astype(jnp.float32)
    return total


def group_send(values):
    count = lax.axis_size("ctx")
    me = lax.axis_index("ctx")
    parts = []
    for shift in range(count):
        block = lax.dynamic_index_in_dim(values, (me + shift) % count, axis=2, keepdims=False)
        if shift:
            pairs = [(i, (i + shift) % count) for i in range(count)]
            block = lax.ppermute(block, "ctx", pairs)
        parts.append(block)
    return jnp.stack(parts)


def group_return(parts):
    count = lax.axis_size("ctx")
    me = lax.axis_index("ctx")
    back = [parts[0]]
    for shift in range(1, count):
        pairs = [(i, (i - shift) % count) for i in range(count)]
        back.append(lax.ppermute(parts[shift], "ctx", pairs))
    stacked = jnp.stack(back)
    order = (jnp.arange(count, dtype=jnp.int32) - me) % count
    return jnp.moveaxis(jnp.take(stacked, order, axis=0), 0, 2)


def gather_axis(values, axis):
    count = lax.axis_size(axis)
    me = lax.axis_index(axis)
    parts = [values]
    for shift in range(1, count):
        pairs = [(i, (i + shift) % count) for i in range(count)]
        parts.append(lax.ppermute(values, axis, pairs))
    stacked = jnp.stack(parts)
    order = (me - jnp.arange(count, dtype=jnp.int32)) % count
    return jnp.take(stacked, order, axis=0)


def small_sum(values):
    every = gather_axis(gather_axis(values, "ctx"), "shard")
    return jnp.sum(every, axis=(0, 1))


def body(
    hidden_in,
    cond,
    scale_len,
    ada_weight,
    ada_bias,
    qkv_weight,
    query_bias,
    value_bias,
    head_scale,
    proj_weight,
    proj_bias,
    up_weight,
    up_bias,
    down_weight,
    down_bias,
    out_grad,
):
    map_count = hidden_in.shape[0]
    piece_rows = hidden_in.shape[1]
    model_width = hidden_in.shape[2]
    ctx_count = lax.axis_size("ctx")
    ctx_index = lax.axis_index("ctx")
    shard_index = lax.axis_index("shard")
    map_length = piece_rows * ctx_count
    heads_here = head_scale.shape[0]
    local_width = query_bias.shape[0]
    head_dim = local_width // heads_here
    row_count = map_count * piece_rows
    head_shape = (map_count, piece_rows, heads_here, head_dim)
    ada_rows = ada_weight.shape[0]
    shard_count = lax.axis_size("shard")
    full_qkv = lax.all_gather(qkv_weight, "shard", axis=0, tiled=True)
    packed = jnp.concatenate(
        [proj_weight.reshape(-1), up_weight.reshape(-1), down_weight.reshape(-1)]
    )
    packed_all = lax.all_gather(packed, "shard", axis=0, tiled=False)
    proj_size, up_size = (proj_weight.size, up_weight.size)
    proj_parts = packed_all[:, :proj_size].reshape((shard_count,) + proj_weight.shape)
    up_parts = packed_all[:, proj_size : proj_size + up_size].reshape(
        (shard_count,) + up_weight.shape
    )
    down_parts = packed_all[:, proj_size + up_size :].reshape((shard_count,) + down_weight.shape)
    full_proj = jnp.transpose(proj_parts, (1, 0, 2)).reshape(proj_weight.shape[0], -1)
    full_up = up_parts.reshape(-1, up_weight.shape[1])
    full_down = jnp.transpose(down_parts, (1, 0, 2)).reshape(down_weight.shape[0], -1)
    qkv_matrix = full_qkv.reshape(model_width, 3 * local_width)
    cond_wide = cond.astype(jnp.float32)
    cond_all = lax.all_gather(cond, "shard", axis=0, tiled=True).astype(jnp.float32)
    cond_in_all = jax.nn.silu(cond_all).astype(jnp.bfloat16)
    cond_cols = lax.dynamic_slice_in_dim(cond_in_all, shard_index * ada_rows, ada_rows, axis=1)
    ada_local = ada_weight.reshape(ada_rows, 6 * model_width)
    mod_partial = jnp.dot(cond_cols, ada_local, preferred_element_type=jnp.float32)
    modulation = lax.psum_scatter(mod_partial, "shard", scatter_dimension=0, tiled=True)
    modulation = modulation.reshape(map_count, 6, model_width) + ada_bias[None]
    gamma_one = modulation[:, 0]
    gamma_two = modulation[:, 1]
    scale_one = modulation[:, 2]
    scale_two = modulation[:, 3]
    shift_one = modulation[:, 4]
    shift_two = modulation[:, 5]
    stream_in = hidden_in.astype(jnp.float32)
    first_mod, first_back = jax.vjp(modulate, stream_in, scale_one, shift_one)
    attn_in = first_mod.astype(jnp.bfloat16).reshape(row_count, model_width)
    qkv = jnp.dot(attn_in, qkv_matrix, preferred_element_type=jnp.float32).reshape(
        map_count, piece_rows, 3, local_width
    )
    query = (qkv[:, :, 0] + query_bias).reshape(head_shape)
    key_raw = qkv[:, :, 1].reshape(head_shape)
    value_low = (qkv[:, :, 2] + value_bias).astype(jnp.bfloat16).reshape(head_shape)
    query_unit, query_back = jax.vjp(unit_scaled, query, head_scale)
    key_unit, key_back = jax.vjp(unit_plain, key_raw)
    query_low = query_unit.astype(jnp.bfloat16)
    key_low = key_unit.astype(jnp.bfloat16)
    group_heads = heads_here // ctx_count
    group_shape = (map_count, piece_rows, ctx_count, group_heads, head_dim)
    query_all = group_send(query_low.reshape(group_shape))
    keys_all = group_send(key_low.reshape(group_shape))
    values_all = group_send(value_low.reshape(group_shape))
    scale_ends = jnp.cumsum(scale_len, axis=1)
    owners = (ctx_index - jnp.arange(ctx_count, dtype=jnp.int32)) % ctx_count
    token_pos = owners[:, None] * piece_rows + jnp.arange(piece_rows, dtype=jnp.int32)[None, :]
    ends = scale_ends[:, None, None, :]
    visible_end = jnp.min(jnp.where(ends > token_pos[None, :, :, None], ends, map_length), axis=3)
    key_mask = token_pos[None, None, None, :, :] < visible_end[:, :, :, None, None]

    def masked_scores():
        raw_scores = jnp.einsum(
            "amqgd,bmkgd->mgaqbk", query_all, keys_all, preferred_element_type=jnp.float32
        )
        return jnp.where(key_mask[:, None], raw_scores, -1e30)

    scores = masked_scores()
    row_max = jnp.max(scores, axis=(-2, -1), keepdims=True)
    exp_scores = jnp.exp(scores - row_max)
    exp_total = jnp.sum(exp_scores, axis=(-2, -1), keepdims=True)
    log_total = row_max + jnp.log(exp_total)
    probs_low = (exp_scores / exp_total).astype(jnp.bfloat16)
    out_all = jnp.einsum(
        "mgaqbk,bmkgd->amqgd", probs_low, values_all, preferred_element_type=jnp.float32
    ).astype(jnp.bfloat16)
    heads_out = group_return(out_all).reshape(row_count, local_width)
    attn_partial = jnp.dot(heads_out, full_proj, preferred_element_type=jnp.float32)
    attn_branch = tp_sum(attn_partial).reshape(map_count, piece_rows, model_width) + proj_bias
    attn_part = gamma_one[:, None] * attn_branch
    mid_stream = stream_in + attn_part
    second_mod, second_back = jax.vjp(modulate, mid_stream, scale_two, shift_two)
    mlp_in = second_mod.astype(jnp.bfloat16).reshape(row_count, model_width)
    pre_act = jnp.dot(mlp_in, full_up, preferred_element_type=jnp.float32) + up_bias
    activation, gelu_back = jax.vjp(gelu_tanh, pre_act)
    act_low = activation.astype(jnp.bfloat16)
    mlp_partial = jnp.dot(act_low, full_down, preferred_element_type=jnp.float32)
    mlp_branch = tp_sum(mlp_partial).reshape(map_count, piece_rows, model_width) + down_bias
    mlp_part = gamma_two[:, None] * mlp_branch
    stream = mid_stream + mlp_part
    grad_top = out_grad.astype(jnp.float32)
    d_gamma_two = jnp.sum(grad_top * mlp_branch, axis=1)
    d_mlp = gamma_two[:, None] * grad_top
    d_down_bias = jnp.sum(d_mlp, axis=(0, 1))
    d_mlp_low = d_mlp.astype(jnp.bfloat16).reshape(row_count, model_width)
    g_down = jnp.einsum("rf,rd->fd", act_low, d_mlp_low, preferred_element_type=jnp.float32)
    d_act = jnp.einsum("rd,fd->rf", d_mlp_low, full_down, preferred_element_type=jnp.float32)
    (d_pre,) = gelu_back(d_act)
    d_up_bias = jnp.sum(d_pre, axis=0)
    d_pre_low = d_pre.astype(jnp.bfloat16)
    g_up = jnp.einsum("rd,rf->df", mlp_in, d_pre_low, preferred_element_type=jnp.float32)
    d_mlp_in_part = jnp.einsum("rf,df->rd", d_pre_low, full_up, preferred_element_type=jnp.float32)
    d_mlp_in = tp_sum(d_mlp_in_part).reshape(map_count, piece_rows, model_width)
    d_mid, d_scale_two, d_shift_two = second_back(d_mlp_in)
    d_mid = d_mid + grad_top
    d_gamma_one = jnp.sum(d_mid * attn_branch, axis=1)
    d_attn = gamma_one[:, None] * d_mid
    d_proj_bias = jnp.sum(d_attn, axis=(0, 1))
    d_attn_low = d_attn.astype(jnp.bfloat16).reshape(row_count, model_width)
    g_proj = jnp.einsum("ri,rd->id", heads_out, d_attn_low, preferred_element_type=jnp.float32)
    d_heads = jnp.einsum("rd,id->ri", d_attn_low, full_proj, preferred_element_type=jnp.float32)
    d_heads = d_heads.astype(jnp.bfloat16).reshape(head_shape)
    d_heads_all = group_send(d_heads.reshape(group_shape))
    probs = probs_low.astype(jnp.float32)
    d_probs = jnp.einsum(
        "amqgd,bmkgd->mgaqbk", d_heads_all, values_all, preferred_element_type=jnp.float32
    )
    row_delta = jnp.sum(probs * d_probs, axis=(-2, -1), keepdims=True)
    d_scores = (probs * (d_probs - row_delta)).astype(jnp.bfloat16)
    probs_again = probs_low
    d_query_all = jnp.einsum(
        "mgaqbk,bmkgd->amqgd", d_scores, keys_all, preferred_element_type=jnp.float32
    ).astype(jnp.bfloat16)
    d_key_all = jnp.einsum(
        "mgaqbk,amqgd->bmkgd", d_scores, query_all, preferred_element_type=jnp.float32
    ).astype(jnp.bfloat16)
    d_value_all = jnp.einsum(
        "mgaqbk,amqgd->bmkgd", probs_again, d_heads_all, preferred_element_type=jnp.float32
    ).astype(jnp.bfloat16)
    d_query_unit = group_return(d_query_all).reshape(head_shape).astype(jnp.float32)
    d_key_unit = group_return(d_key_all).reshape(head_shape).astype(jnp.float32)
    d_value = group_return(d_value_all).reshape(head_shape).astype(jnp.float32)
    d_query, d_head_scale = query_back(d_query_unit)
    (d_key,) = key_back(d_key_unit)
    d_query = d_query.reshape(map_count, piece_rows, local_width)
    d_key = d_key.reshape(map_count, piece_rows, local_width)
    d_value = d_value.reshape(map_count, piece_rows, local_width)
    d_query_bias = jnp.sum(d_query, axis=(0, 1))
    d_value_bias = jnp.sum(d_value, axis=(0, 1))
    d_qkv = (
        jnp.stack([d_query, d_key, d_value], axis=2)
        .astype(jnp.bfloat16)
        .reshape(row_count, 3 * local_width)
    )
    g_qkv = jnp.einsum("rd,rc->dc", attn_in, d_qkv, preferred_element_type=jnp.float32).reshape(
        model_width, 3, local_width
    )
    d_attn_in_part = jnp.einsum("rc,dc->rd", d_qkv, qkv_matrix, preferred_element_type=jnp.float32)
    d_attn_in = tp_sum(d_attn_in_part).reshape(map_count, piece_rows, model_width)
    d_input, d_scale_one, d_shift_one = first_back(d_attn_in)
    d_input = d_input + d_mid
    d_mod_part = jnp.stack(
        [d_gamma_one, d_gamma_two, d_scale_one, d_scale_two, d_shift_one, d_shift_two], axis=1
    )
    d_mod = lax.psum(d_mod_part, "ctx").astype(jnp.bfloat16).reshape(map_count, 6 * model_width)
    d_mod_all = lax.all_gather(d_mod, "shard", axis=0, tiled=True)
    g_ada = jnp.einsum(
        "md,mc->dc", cond_cols, d_mod_all, preferred_element_type=jnp.float32
    ).reshape(ada_rows, 6, model_width)
    d_ada_bias = jnp.sum(d_mod_all.astype(jnp.float32), axis=0).reshape(6, model_width)
    d_cond_cols = jnp.einsum("mc,dc->md", d_mod_all, ada_local, preferred_element_type=jnp.float32)
    d_cond_in = lax.all_to_all(d_cond_cols, "shard", 0, 1, tiled=True)
    silu_value, silu_back = jax.vjp(jax.nn.silu, cond_wide)
    (d_cond,) = silu_back(d_cond_in)
    early_shards = (
        lax.psum_scatter(g_up.astype(jnp.bfloat16), "shard", scatter_dimension=0, tiled=True),
        lax.psum_scatter(g_proj.astype(jnp.bfloat16), "shard", scatter_dimension=1, tiled=True),
        lax.psum_scatter(g_down.astype(jnp.bfloat16), "shard", scatter_dimension=1, tiled=True),
    )
    early_summed = lax.psum(early_shards, "ctx")
    qkv_low, early_summed = lax.optimization_barrier((g_qkv.astype(jnp.bfloat16), early_summed))
    qkv_shard = lax.psum_scatter(qkv_low, "shard", scatter_dimension=0, tiled=True)
    qkv_summed = lax.psum(qkv_shard, "ctx")
    summed = tuple(
        (
            g.astype(jnp.float32)
            for g in (qkv_summed, early_summed[0], early_summed[1], early_summed[2])
        )
    )
    square_sums = jnp.stack(
        [jnp.sum(stream * stream), jnp.sum(attn_part * attn_part), jnp.sum(mlp_part * mlp_part)]
    )
    small_parts = (
        square_sums,
        d_query_bias,
        d_value_bias,
        d_head_scale,
        d_proj_bias,
        d_up_bias,
        d_down_bias,
    )
    small_flat = small_sum(jnp.concatenate(small_parts))
    small = []
    offset = 0
    for part in small_parts:
        small.append(small_flat[offset : offset + part.shape[0]])
        offset += part.shape[0]
    entry_total = map_count * map_length * model_width * lax.axis_size("shard")
    norm_stats = jnp.sqrt(small[0] / entry_total)
    return (
        stream.astype(jnp.bfloat16),
        d_input.astype(jnp.bfloat16),
        d_cond,
        g_ada,
        d_ada_bias,
        summed[0],
        small[1],
        small[2],
        small[3],
        summed[2],
        small[4],
        summed[1],
        small[5],
        summed[3],
        small[6],
        norm_stats,
    )


def solution(mesh):
    in_specs = (
        P("shard", "ctx", None),
        P("shard", None),
        P("shard", None),
        P("shard", None, None),
        P(),
        P("shard", None, "tp"),
        P("tp"),
        P("tp"),
        P("tp"),
        P("tp", "shard"),
        P(),
        P("shard", "tp"),
        P("tp"),
        P("tp", "shard"),
        P(),
        P("shard", "ctx", None),
    )
    out_specs = (
        P("shard", "ctx", None),
        P("shard", "ctx", None),
        P("shard", None),
        P("shard", None, None),
        P(),
        P("shard", None, "tp"),
        P("tp"),
        P("tp"),
        P("tp"),
        P("tp", "shard"),
        P(),
        P("shard", "tp"),
        P("tp"),
        P("tp", "shard"),
        P(),
        P(),
    )
    return jax.shard_map(body, mesh=mesh, in_specs=in_specs, out_specs=out_specs, check_vma=False)
```

profile of v0, /device:TPU:0, one launch (start us, length us, event | category | flops | bytes accessed | tf_op | source)
XLA Modules:
  0.0 849.8 jit_solution(5357631159717462529)
XLA Ops:
  9.6 15.1 %all-gather.1 = bf16[4,6,1024]{2,1,0:T(8,128)(2,1)S(1)} all-gather(bf16[1,6,1024]{2,1,0:T(8,128)(2,1)} %bitcast.391), channel_id=1, replica_groups=mesh['shard'=4,'ctx'=4,'tp'=2] {'shard'}, dimensions={0}, use_global_device_ids=true | all-gather | bytes 61440 | tf_op jit(solution)/shard_map/all_gather | solution.py:145
  29.9 33.7 %fusion = f32[8,6144]{1,0:T(8,128)S(1)} fusion(f32[24,6144]{1,0:T(8,128)} %fusion.65), kind=kCustom, calls=%all-reduce-scatter | all-reduce-scatter fusion | flops 196609 | bytes 786944
  71.8 10.8 %pad_maximum_fusion = bf16[1179648]{0:T(1024)(128)(2,1)} fusion(bf16[524288]{0:T(1024)(128)(2,1)S(1)} %bitcast.361, bf16[524288]{0:T(1024)(128)(2,1)S(1)} %bitcast.360, bf16[131072]{0:T(1024)(128)(2,1)S(1)} %bitcast.371), kind=kLoop, calls=%fused_computation.87 | loop fusion | flops 7077888 | bytes 4718592 | tf_op jit(solution)/shard_map/concatenate | solution.py:130
  153.9 17.3 %select_reduce_fusion = (f32[6,2,4,170]{3,2,1,0:T(4,128)S(1)}, f32[6,2,4,170,4,170]{3,5,4,2,1,0:T(8,128)}) fusion(pred[6,4,170,4,170]{2,4,3,1,0:T(8,128)(4,1)} %broadcast_compare_fusion, bf16[1,6,170,2,64]{2,4,0,3,1:T(8,128)(2,1)} %bitcast.37, bf16[1,6,170,2,64]{2,4,0,3,1:T(8,128)(2,1)} %bitcast.35, bf16[1,6,170,2,64]{2,4,0,3,1:T(8,128)(2,1)} %bitcast.33, ...), kind=kOutput, calls=%fused_computation.12 | convolution fusion | flops 729691648 | bytes 27091200 | tf_op jit(solution)/shard_map/amqgd,bmkgd->mgaqbk/dot_general | solution.py:184
  171.3 15.7 %fusion.3 = f32[6,2,4,170]{3,2,1,0:T(4,128)S(1)} fusion(f32[6,2,4,170,4,170]{3,5,4,2,1,0:T(8,128)} %get-tuple-element.186, f32[6,2,4,170]{3,2,1,0:T(4,128)S(1)} %get-tuple-element.185, pred[6,4,170,4,170]{2,4,3,1,0:T(8,128)(4,1)} %broadcast_compare_fusion), kind=kLoop, calls=%fused_computation.13 | loop fusion | flops 16638240 | bytes 25034880 | tf_op jit(solution)/shard_map/reduce_sum | solution.py:192
  193.7 12.2 %divide_convert_fusion = bf16[6,2,4,170,4,170]{3,5,4,2,1,0:T(8,128)(2,1)} fusion(f32[6,2,4,170,4,170]{3,5,4,2,1,0:T(8,128)S(1)} %copy-done, f32[6,2,4,170]{3,2,1,0:T(4,128)S(1)} %fusion.3, f32[6,2,4,170]{3,2,1,0:T(4,128)S(1)} %get-tuple-element.185, pred[6,4,170,4,170]{2,4,3,1,0:T(8,128)(4,1)} %broadcast_compare_fusion), kind=kLoop, calls=%fused_computation.10 | loop fusion | flops 22195200 | bytes 36132480 | tf_op jit(solution)/shard_map/convert_element_type | solution.py:194
  205.9 9.6 %fusion.35 = bf16[4,6,170,2,64]{2,4,0,3,1:T(8,128)(2,1)S(1)} fusion(bf16[6,2,4,170,4,170]{3,5,4,2,1,0:T(8,128)(2,1)} %divide_convert_fusion, bf16[1,6,170,2,64]{2,4,0,3,1:T(8,128)(2,1)} %bitcast.15, bf16[1,6,170,2,64]{2,4,0,3,1:T(8,128)(2,1)} %bitcast.13, bf16[1,6,170,2,64]{2,4,0,3,1:T(8,128)(2,1)} %bitcast.11, ...), kind=kOutput, calls=%fused_computation.107 | convolution fusion | flops 714946560 | bytes 13186560 | tf_op jit(solution)/shard_map/mgaqbk,bmkgd->amqgd/dot_general | solution.py:195
  241.0 18.9 %all-gather.8.cloned.1.call-done = bf16[4718592]{0:T(1024)(128)(2,1)} async-done(((bf16[1179648]{0:T(1024)(128)(2,1)}), bf16[4718592]{0:T(1024)(128)(2,1)}) %all-gather.8.cloned.1.call-update) | async-done | bytes 9437200 | tf_op jit(solution)/shard_map/all_gather | solution.py:133
  259.9 12.5 %reshape.660 = bf16[4,1179648]{1,0:T(4,128)(2,1)} reshape(bf16[4718592]{0:T(1024)(128)(2,1)} %all-gather.8.cloned.1.call-done) | data formatting | bytes 18874368 | tf_op jit(solution)/shard_map/all_gather | solution.py:133
  278.0 8.3 fusion.72
  286.4 8.0 reshape_reshape.7
  305.6 9.2 %multiply_reduce_fusion.6 = (f32[]{:T(128)}, f32[1020,1024]{1,0:T(8,128)}) fusion(f32[1020,1024]{1,0:T(8,128)} %mul.528, f32[1024]{0:T(1024)S(1)} %copy-done.76, f32[1020,1024]{1,0:T(8,128)} %fusion.76, f32[1020,1024]{1,0:T(8,128)} %collective-permute-done.12), kind=kLoop, calls=%fused_computation.58 | loop fusion | flops 5222399 | bytes 16715780 | tf_op jit(solution)/shard_map/reduce_sum | solution.py:302
  327.9 7.5 fusion.77
  335.5 10.6 %fusion.69 = (f32[2048]{0:T(1024)}, bf16[1020,2048]{1,0:T(8,128)(2,1)S(1)}) fusion(f32[1020,2048]{1,0:T(8,128)S(1)} %fusion.77, f32[2048]{0:T(1024)S(1)} %copy-done.97, bf16[1020,1024]{1,0:T(8,128)(2,1)S(1)} %copy-done.30, bf16[2048,1024]{0,1:T(8,128)(2,1)S(1)} %bitcast.356), kind=kOutput, calls=%fused_computation.244 | convolution fusion | flops 4324145152 | bytes 18833408 | tf_op jit(solution)/shard_map/rd,fd->rf/dot_general | solution.py:218
  352.8 6.9 fusion.67
  377.4 9.3 %multiply_reduce_fusion.5 = (f32[]{:T(128)}, f32[1020,1024]{1,0:T(8,128)}) fusion(f32[1020,1024]{1,0:T(8,128)} %mul.531, f32[1024]{0:T(1024)S(1)} %copy-done.85, f32[1020,1024]{1,0:T(8,128)} %fusion.67, f32[1020,1024]{1,0:T(8,128)} %collective-permute-done.13), kind=kLoop, calls=%fused_computation.57 | loop fusion | flops 5222399 | bytes 16715780 | tf_op jit(solution)/shard_map/reduce_sum | solution.py:302
  391.0 8.4 multiply_reduce_fusion
  417.2 8.3 convolution_convert_fusion.1
  442.7 11.9 %convolution_convert_fusion = bf16[2048,1024]{1,0:T(8,128)(2,1)} fusion(bf16[1020,1024]{1,0:T(8,128)(2,1)S(1)} %copy-done.31, f32[1020,2048]{1,0:T(8,128)} %copy-done.102, f32[2048]{0:T(1024)S(1)} %copy-done.98), kind=kOutput, calls=%fused_computation.65 | convolution fusion | flops 4301176832 | bytes 14647296 | tf_op jit(solution)/shard_map/rf,rd->fd/dot_general | solution.py:217
  460.0 11.7 %fusion.38 = bf16[4,6,170,2,64]{2,4,0,3,1:T(8,128)(2,1)S(1)} fusion(bf16[6,2,4,170,4,170]{3,5,4,2,1,0:T(8,128)(2,1)} %divide_convert_fusion, bf16[1,6,170,2,64]{2,4,0,3,1:T(8,128)(2,1)} %bitcast.369, bf16[1,6,170,2,64]{2,4,0,3,1:T(8,128)(2,1)S(1)} %bitcast.367, bf16[1,6,170,2,64]{2,4,0,3,1:T(8,128)(2,1)S(1)} %bitcast.365, ...), kind=kOutput, calls=%fused_computation.110 | convolution fusion | flops 714946560 | bytes 13186560 | tf_op jit(solution)/shard_map/mgaqbk,amqgd->bmkgd/dot_general | solution.py:248
  471.7 18.4 %fusion.1 = (f32[6,2,4,170]{3,2,1,0:T(4,128)S(1)}, f32[6,2,4,170,4,170]{3,5,4,2,1,0:T(8,128)}) fusion(bf16[6,2,4,170,4,170]{3,5,4,2,1,0:T(8,128)(2,1)} %divide_convert_fusion, bf16[1,6,170,2,64]{2,4,0,3,1:T(8,128)(2,1)} %bitcast.15, bf16[1,6,170,2,64]{2,4,0,3,1:T(8,128)(2,1)} %bitcast.13, bf16[1,6,170,2,64]{2,4,0,3,1:T(8,128)(2,1)} %bitcast.11, ...), kind=kOutput, calls=%fused_computation.8 | convolution fusion | flops 735240448 | bytes 35414400 | tf_op jit(solution)/shard_map/amqgd,bmkgd->mgaqbk/dot_general | solution.py:236
  494.6 23.8 %fusion.2 = bf16[6,2,4,170,4,170]{3,5,4,2,1,0:T(8,128)(2,1)S(1)} fusion(f32[6,2,4,170,4,170]{3,5,4,2,1,0:T(8,128)} %get-tuple-element.188, f32[6,2,4,170]{3,2,1,0:T(4,128)S(1)} %get-tuple-element.187, f32[6,2,4,170]{3,2,1,0:T(4,128)S(1)} %copy-done.55, f32[6,2,4,170]{3,2,1,0:T(4,128)S(1)} %copy-done.53, f32[6,2,4,170,4,170]{3,5,4,2,1,0:T(8,128)} %get-tuple-element.186, ...), kind=kLoop, calls=%fused_computation.9 | loop fusion | flops 44390400 | bytes 58360320 | tf_op jit(solution)/shard_map/convert_element_type | solution.py:240
  528.8 12.4 %fusion.37 = bf16[4,6,170,2,64]{2,4,0,3,1:T(8,128)(2,1)S(1)} fusion(bf16[6,2,4,170,4,170]{3,5,4,2,1,0:T(8,128)(2,1)} %copy-done.1, bf16[1,6,170,2,64]{2,4,0,3,1:T(8,128)(2,1)} %bitcast.381, bf16[1,6,170,2,64]{2,4,0,3,1:T(8,128)(2,1)} %bitcast.383, bf16[1,6,170,2,64]{2,4,0,3,1:T(8,128)(2,1)} %bitcast.385, bf16[1,6,170,2,64]{2,4,0,3,1:T(8,128)(2,1)} %get-tuple-element.162), kind=kOutput, calls=%fused_computation.109 | convolution fusion | flops 714946560 | bytes 13186560 | tf_op jit(solution)/shard_map/mgaqbk,amqgd->bmkgd/dot_general | solution.py:245
  556.5 7.3 collective-permute-done.23
  571.8 7.2 collective-permute-done.20
  634.9 9.1 %add_add_fusion.4 = (bf16[6,170,1,512]{3,1,2,0:T(8,128)(2,1)}, bf16[6,170,1,512]{3,1,2,0:T(8,128)(2,1)}) fusion(f32[6,170,1,512]{3,1,2,0:T(8,128)} %copy.255, f32[6,170,1,512]{3,1,2,0:T(8,128)} %copy.253, f32[6,170,1,512]{3,1,2,0:T(8,128)S(1)} %copy-done.18, f32[512]{0:T(512)S(1)} %copy-done.80, f32[512]{0:T(512)S(1)} %mul.494, ...), kind=kLoop, calls=%fused_computation.68 | loop fusion | flops 6266880 | bytes 18804736 | tf_op jit(solution)/shard_map/transpose(jvp())/add_any | solution.py:18
  654.5 7.0 fusion.78
  667.4 47.9 %all-reduce.9.cloned.1.call-done = (bf16[256,2048]{1,0:T(8,128)(2,1)}, bf16[512,256]{1,0:T(8,128)(2,1)}, bf16[2048,256]{1,0:T(8,128)(2,1)}) async-done(((bf16[256,2048]{1,0:T(8,128)(2,1)}, bf16[512,256]{1,0:T(8,128)(2,1)}, bf16[2048,256]{1,0:T(8,128)(2,1)}), (bf16[256,2048]{1,0:T(8,128)(2,1)}, bf16[512,256]{1,0:T(8,128)(2,1)}, bf16[2048,256]{1,0:T(8,128)(2,1)})) %all-reduce.9.cloned.1.call-update) | async-done | bytes 2359312 | tf_op jit(solution)/shard_map/psum | solution.py:291
  730.6 6.9 add.451
  747.9 19.0 %all-reduce.10 = bf16[6,6,1024]{2,1,0:T(8,128)(2,1)S(1)} all-reduce(f32[6,6,1024]{2,1,0:T(8,128)S(1)} %stack.200), channel_id=1, replica_groups=mesh['shard'=4,'ctx'=4,'tp'=2] {'ctx'}, use_global_device_ids=true, to_apply=%region_24.26 | all-reduce | flops 36864 | bytes 221184 | tf_op jit(solution)/shard_map/psum | solution.py:276
  766.9 21.6 %all-gather.2 = bf16[4,6,6144]{2,1,0:T(8,128)(2,1)S(1)} all-gather(bf16[1,6,6144]{2,1,0:T(8,128)(2,1)S(1)} %reshape.667), channel_id=1, replica_groups=mesh['shard'=4,'ctx'=4,'tp'=2] {'shard'}, dimensions={0}, use_global_device_ids=true | all-gather | bytes 368640 | tf_op jit(solution)/shard_map/all_gather | solution.py:277
  816.7 23.3 %all-reduce.7.cloned.1.call-done = bf16[256,3,512]{2,0,1:T(8,128)(2,1)} async-done(((bf16[256,3,512]{2,0,1:T(8,128)(2,1)}), bf16[256,3,512]{2,0,1:T(8,128)(2,1)}) %all-reduce.7.cloned.1.call-update) | async-done | bytes 786448 | tf_op jit(solution)/shard_map/psum | solution.py:294
  (493 shorter events, 383.0 us)
Async XLA Ops:
  7.2 90.3 %all-gather.6.cloned.1.call-start = ((), (), s32[]{:S(2)}) async-start(), calls=%async_computation.5 | async-start | bytes 3932160 | tf_op jit(solution)/shard_map/all_gather | solution.py:129
  9.5 250.4 %all-gather.8.cloned.1.call-start = ((), (), s32[]{:S(2)}) async-start(), calls=%async_computation.11 | async-start | bytes 11796480 | tf_op jit(solution)/shard_map/all_gather | solution.py:133
  63.6 29.0 %collective-permute-start.34 = (f32[6,6144]{1,0:T(8,128)S(1)}, f32[6,6144]{1,0:T(8,128)}, u32[]{:S(2)}, u32[]{:S(2)}) collective-permute-start(f32[6,6144]{1,0:T(8,128)S(1)} %slice.187), channel_id=1, source_target_pairs={{0,8},{8,16},{16,24},{1,9},{9,17},{17,25},{2,10},{10,18},{18,26},{... | collective-permute-start | bytes 442376
  82.7 561.3 %reduce-scatter.9.cloned.1.call-start = ((), (), s32[]{:S(2)}) async-start(), calls=%async_computation.7 | async-start | bytes 1310720 | tf_op jit(solution)/shard_map/reduce_scatter | solution.py:288
  117.8 19.5 %collective-permute-start.7 = (bf16[6,170,2,64]{1,3,2,0:T(8,128)(2,1)}, bf16[6,170,2,64]{1,3,2,0:T(8,128)(2,1)}, u32[]{:S(2)}, u32[]{:S(2)}) collective-permute-start(bf16[6,170,2,64]{1,3,2,0:T(8,128)(2,1)} %get-tuple-element.168), channel_id=1, source_target_pairs={{0,4},{2,6},{4,0},{6,2},{1,5},{3,7},{5,1},{7,3},{8,12},{10,14},{12... | collective-permute-start | bytes 783368 | tf_op jit(solution)/shard_map/ppermute | solution.py:63
  118.3 20.8 %collective-permute-start.6 = (bf16[6,170,2,64]{1,3,2,0:T(8,128)(2,1)}, bf16[6,170,2,64]{1,3,2,0:T(8,128)(2,1)}, u32[]{:S(2)}, u32[]{:S(2)}) collective-permute-start(bf16[6,170,2,64]{1,3,2,0:T(8,128)(2,1)} %get-tuple-element.169), channel_id=1, source_target_pairs={{0,2},{2,4},{4,6},{6,0},{1,3},{3,5},{5,7},{7,1},{8,10},{10,12},{12... | collective-permute-start | bytes 783368 | tf_op jit(solution)/shard_map/ppermute | solution.py:63
  124.6 19.9 %collective-permute-start.5 = (bf16[6,170,2,64]{1,3,2,0:T(8,128)(2,1)S(1)}, bf16[6,170,2,64]{1,3,2,0:T(8,128)(2,1)S(1)}, u32[]{:S(2)}, u32[]{:S(2)}) collective-permute-start(bf16[6,170,2,64]{1,3,2,0:T(8,128)(2,1)S(1)} %get-tuple-element.163), channel_id=1, source_target_pairs={{0,6},{2,0},{4,2},{6,4},{1,7},{3,1},{5,3},{7,5},{8,14},{10,8},{12,... | collective-permute-start | bytes 783368 | tf_op jit(solution)/shard_map/ppermute | solution.py:63
  126.9 25.8 %collective-permute-start.4 = (bf16[6,170,2,64]{1,3,2,0:T(8,128)(2,1)S(1)}, bf16[6,170,2,64]{1,3,2,0:T(8,128)(2,1)S(1)}, u32[]{:S(2)}, u32[]{:S(2)}) collective-permute-start(bf16[6,170,2,64]{1,3,2,0:T(8,128)(2,1)S(1)} %get-tuple-element.164), channel_id=1, source_target_pairs={{0,4},{2,6},{4,0},{6,2},{1,5},{3,7},{5,1},{7,3},{8,12},{10,14},{12... | collective-permute-start | bytes 783368 | tf_op jit(solution)/shard_map/ppermute | solution.py:63
  128.5 25.5 %collective-permute-start.3 = (bf16[6,170,2,64]{1,3,2,0:T(8,128)(2,1)S(1)}, bf16[6,170,2,64]{1,3,2,0:T(8,128)(2,1)S(1)}, u32[]{:S(2)}, u32[]{:S(2)}) collective-permute-start(bf16[6,170,2,64]{1,3,2,0:T(8,128)(2,1)S(1)} %get-tuple-element.165), channel_id=1, source_target_pairs={{0,2},{2,4},{4,6},{6,0},{1,3},{3,5},{5,7},{7,1},{8,10},{10,12},{12... | collective-permute-start | bytes 783368 | tf_op jit(solution)/shard_map/ppermute | solution.py:63
  137.2 68.7 %collective-permute-start.2 = (bf16[6,170,2,64]{1,3,2,0:T(8,128)(2,1)}, bf16[6,170,2,64]{1,3,2,0:T(8,128)(2,1)}, u32[]{:S(2)}, u32[]{:S(2)}) collective-permute-start(bf16[6,170,2,64]{1,3,2,0:T(8,128)(2,1)} %get-tuple-element.159), channel_id=1, source_target_pairs={{0,6},{2,0},{4,2},{6,4},{1,7},{3,1},{5,3},{7,5},{8,14},{10,8},{12,... | collective-permute-start | bytes 783368 | tf_op jit(solution)/shard_map/ppermute | solution.py:63
  139.1 66.9 %collective-permute-start.1 = (bf16[6,170,2,64]{1,3,2,0:T(8,128)(2,1)}, bf16[6,170,2,64]{1,3,2,0:T(8,128)(2,1)}, u32[]{:S(2)}, u32[]{:S(2)}) collective-permute-start(bf16[6,170,2,64]{1,3,2,0:T(8,128)(2,1)} %get-tuple-element.160), channel_id=1, source_target_pairs={{0,4},{2,6},{4,0},{6,2},{1,5},{3,7},{5,1},{7,3},{8,12},{10,14},{12... | collective-permute-start | bytes 783368 | tf_op jit(solution)/shard_map/ppermute | solution.py:63
  144.5 61.5 %collective-permute-start = (bf16[6,170,2,64]{1,3,2,0:T(8,128)(2,1)}, bf16[6,170,2,64]{1,3,2,0:T(8,128)(2,1)}, u32[]{:S(2)}, u32[]{:S(2)}) collective-permute-start(bf16[6,170,2,64]{1,3,2,0:T(8,128)(2,1)} %get-tuple-element.161), channel_id=1, source_target_pairs={{0,2},{2,4},{4,6},{6,0},{1,3},{3,5},{5,7},{7,1},{8,10},{10,12},{12... | collective-permute-start | bytes 783368 | tf_op jit(solution)/shard_map/ppermute | solution.py:63
  278.0 27.5 %collective-permute-start.12 = (f32[1020,1024]{1,0:T(8,128)}, f32[1020,1024]{1,0:T(8,128)}, u32[]{:S(2)}, u32[]{:S(2)}) collective-permute-start(f32[1020,1024]{1,0:T(8,128)} %fusion.76), channel_id=1, source_target_pairs={{0,1},{1,0},{2,3},{3,2},{4,5},{5,4},{6,7},{7,6},{8,9},{9,8},{10,11... | collective-permute-start | bytes 12533768 | tf_op jit(solution)/shard_map/ppermute | solution.py:34
  417.2 226.8 %reduce-scatter.7.cloned.1.call-start = ((), (), s32[]{:S(2)}) async-start(), calls=%async_computation.6 | async-start | bytes 5242880 | tf_op jit(solution)/shard_map/reduce_scatter | solution.py:287
  425.6 218.4 %reduce-scatter.11.cloned.1.call-start = ((), (), s32[]{:S(2)}) async-start(), calls=%async_computation.8 | async-start | bytes 5242880 | tf_op jit(solution)/shard_map/reduce_scatter | solution.py:289
  438.3 18.9 %collective-permute-start.15 = (bf16[6,170,2,64]{1,3,2,0:T(8,128)(2,1)S(1)}, bf16[6,170,2,64]{1,3,2,0:T(8,128)(2,1)S(1)}, u32[]{:S(2)}, u32[]{:S(2)}) collective-permute-start(bf16[6,170,2,64]{1,3,2,0:T(8,128)(2,1)S(1)} %bitcast.378), channel_id=1, source_target_pairs={{0,2},{2,4},{4,6},{6,0},{1,3},{3,5},{5,7},{7,1},{8,10},{10,12},{12... | collective-permute-start | bytes 783368 | tf_op jit(solution)/shard_map/ppermute | solution.py:63
  439.8 19.4 %collective-permute-start.16 = (bf16[6,170,2,64]{1,3,2,0:T(8,128)(2,1)S(1)}, bf16[6,170,2,64]{1,3,2,0:T(8,128)(2,1)S(1)}, u32[]{:S(2)}, u32[]{:S(2)}) collective-permute-start(bf16[6,170,2,64]{1,3,2,0:T(8,128)(2,1)S(1)} %bitcast.377), channel_id=1, source_target_pairs={{0,4},{2,6},{4,0},{6,2},{1,5},{3,7},{5,1},{7,3},{8,12},{10,14},{12... | collective-permute-start | bytes 783368 | tf_op jit(solution)/shard_map/ppermute | solution.py:63
  441.3 18.0 %collective-permute-start.17 = (bf16[6,170,2,64]{1,3,2,0:T(8,128)(2,1)S(1)}, bf16[6,170,2,64]{1,3,2,0:T(8,128)(2,1)S(1)}, u32[]{:S(2)}, u32[]{:S(2)}) collective-permute-start(bf16[6,170,2,64]{1,3,2,0:T(8,128)(2,1)S(1)} %bitcast.376), channel_id=1, source_target_pairs={{0,6},{2,0},{4,2},{6,4},{1,7},{3,1},{5,3},{7,5},{8,14},{10,8},{12,... | collective-permute-start | bytes 783368 | tf_op jit(solution)/shard_map/ppermute | solution.py:63
  454.6 260.7 %all-reduce.9.cloned.1.call-start = ((), (), s32[]{:S(2)}) async-start(), calls=%async_computation.12 | async-start | bytes 4718592 | tf_op jit(solution)/shard_map/psum | solution.py:291
  491.2 55.1 %collective-permute-start.24 = (bf16[6,170,2,64]{1,3,2,0:T(8,128)(2,1)}, bf16[6,170,2,64]{1,3,2,0:T(8,128)(2,1)}, u32[]{:S(2)}, u32[]{:S(2)}) collective-permute-start(bf16[6,170,2,64]{1,3,2,0:T(8,128)(2,1)} %get-tuple-element.151), channel_id=1, source_target_pairs={{0,6},{2,0},{4,2},{6,4},{1,7},{3,1},{5,3},{7,5},{8,14},{10,8},{12,... | collective-permute-start | bytes 783368 | tf_op jit(solution)/shard_map/ppermute | solution.py:74
  492.8 54.0 %collective-permute-start.26 = (bf16[6,170,2,64]{1,3,2,0:T(8,128)(2,1)}, bf16[6,170,2,64]{1,3,2,0:T(8,128)(2,1)}, u32[]{:S(2)}, u32[]{:S(2)}) collective-permute-start(bf16[6,170,2,64]{1,3,2,0:T(8,128)(2,1)} %get-tuple-element.152), channel_id=1, source_target_pairs={{0,2},{2,4},{4,6},{6,0},{1,3},{3,5},{5,7},{7,1},{8,10},{10,12},{12... | collective-permute-start | bytes 783368 | tf_op jit(solution)/shard_map/ppermute | solution.py:74
  493.2 56.5 %collective-permute-start.25 = (bf16[6,170,2,64]{1,3,2,0:T(8,128)(2,1)}, bf16[6,170,2,64]{1,3,2,0:T(8,128)(2,1)}, u32[]{:S(2)}, u32[]{:S(2)}) collective-permute-start(bf16[6,170,2,64]{1,3,2,0:T(8,128)(2,1)} %get-tuple-element.153), channel_id=1, source_target_pairs={{0,4},{2,6},{4,0},{6,2},{1,5},{3,7},{5,1},{7,3},{8,12},{10,14},{12... | collective-permute-start | bytes 783368 | tf_op jit(solution)/shard_map/ppermute | solution.py:74
  546.2 20.8 %collective-permute-start.22 = (bf16[6,170,2,64]{1,3,2,0:T(8,128)(2,1)}, bf16[6,170,2,64]{1,3,2,0:T(8,128)(2,1)}, u32[]{:S(2)}, u32[]{:S(2)}) collective-permute-start(bf16[6,170,2,64]{1,3,2,0:T(8,128)(2,1)} %get-tuple-element.149), channel_id=1, source_target_pairs={{0,4},{2,6},{4,0},{6,2},{1,5},{3,7},{5,1},{7,3},{8,12},{10,14},{12... | collective-permute-start | bytes 783368 | tf_op jit(solution)/shard_map/ppermute | solution.py:74
  546.8 25.0 %collective-permute-start.18 = (bf16[6,170,2,64]{1,3,2,0:T(8,128)(2,1)}, bf16[6,170,2,64]{1,3,2,0:T(8,128)(2,1)}, u32[]{:S(2)}, u32[]{:S(2)}) collective-permute-start(bf16[6,170,2,64]{1,3,2,0:T(8,128)(2,1)} %get-tuple-element.143), channel_id=1, source_target_pairs={{0,6},{2,0},{4,2},{6,4},{1,7},{3,1},{5,3},{7,5},{8,14},{10,8},{12,... | collective-permute-start | bytes 783368 | tf_op jit(solution)/shard_map/ppermute | solution.py:74
  549.7 29.3 %collective-permute-start.20 = (bf16[6,170,2,64]{1,3,2,0:T(8,128)(2,1)}, bf16[6,170,2,64]{1,3,2,0:T(8,128)(2,1)}, u32[]{:S(2)}, u32[]{:S(2)}) collective-permute-start(bf16[6,170,2,64]{1,3,2,0:T(8,128)(2,1)} %get-tuple-element.144), channel_id=1, source_target_pairs={{0,2},{2,4},{4,6},{6,0},{1,3},{3,5},{5,7},{7,1},{8,10},{10,12},{12... | collective-permute-start | bytes 783368 | tf_op jit(solution)/shard_map/ppermute | solution.py:74
  554.9 26.6 %collective-permute-start.19 = (bf16[6,170,2,64]{1,3,2,0:T(8,128)(2,1)}, bf16[6,170,2,64]{1,3,2,0:T(8,128)(2,1)}, u32[]{:S(2)}, u32[]{:S(2)}) collective-permute-start(bf16[6,170,2,64]{1,3,2,0:T(8,128)(2,1)} %get-tuple-element.145), channel_id=1, source_target_pairs={{0,4},{2,6},{4,0},{6,2},{1,5},{3,7},{5,1},{7,3},{8,12},{10,14},{12... | collective-permute-start | bytes 783368 | tf_op jit(solution)/shard_map/ppermute | solution.py:74
  610.9 55.6 %collective-permute-start.30 = (f32[5131]{0:T(1024)S(1)}, f32[5131]{0:T(1024)S(1)}, u32[]{:S(2)}, u32[]{:S(2)}) collective-permute-start(f32[5131]{0:T(1024)S(1)} %concatenate.7), channel_id=1, source_target_pairs={{0,6},{2,0},{4,2},{6,4},{1,7},{3,1},{5,3},{7,5},{8,14},{10,8},{12,... | collective-permute-start | bytes 61580 | tf_op jit(solution)/shard_map/ppermute | solution.py:86
  611.0 55.5 %collective-permute-start.29 = (f32[5131]{0:T(1024)S(1)}, f32[5131]{0:T(1024)S(1)}, u32[]{:S(2)}, u32[]{:S(2)}) collective-permute-start(f32[5131]{0:T(1024)S(1)} %concatenate.7), channel_id=1, source_target_pairs={{0,4},{2,6},{4,0},{6,2},{1,5},{3,7},{5,1},{7,3},{8,12},{10,14},{12... | collective-permute-start | bytes 61580 | tf_op jit(solution)/shard_map/ppermute | solution.py:86
  611.6 54.9 %collective-permute-start.28 = (f32[5131]{0:T(1024)S(1)}, f32[5131]{0:T(1024)S(1)}, u32[]{:S(2)}, u32[]{:S(2)}) collective-permute-start(f32[5131]{0:T(1024)S(1)} %concatenate.7), channel_id=1, source_target_pairs={{0,2},{2,4},{4,6},{6,0},{1,3},{3,5},{5,7},{7,1},{8,10},{10,12},{12... | collective-permute-start | bytes 61580 | tf_op jit(solution)/shard_map/ppermute | solution.py:86
  644.0 149.8 %reduce-scatter.13.cloned.1.call-start = ((), (), s32[]{:S(2)}) async-start(), calls=%async_computation.9 | async-start | bytes 3932160 | tf_op jit(solution)/shard_map/reduce_scatter | solution.py:293
  661.5 69.1 %collective-permute-start.27 = (f32[1020,1024]{1,0:T(8,128)}, f32[1020,1024]{1,0:T(8,128)}, u32[]{:S(2)}, u32[]{:S(2)}) collective-permute-start(f32[1020,1024]{1,0:T(8,128)} %fusion.78), channel_id=1, source_target_pairs={{0,1},{1,0},{2,3},{3,2},{4,5},{5,4},{6,7},{7,6},{8,9},{9,8},{10,11... | collective-permute-start | bytes 12533768 | tf_op jit(solution)/shard_map/ppermute | solution.py:34
  715.4 124.6 %all-reduce.7.cloned.1.call-start = ((), (), s32[]{:S(2)}) async-start(), calls=%async_computation.10 | async-start | bytes 1572864 | tf_op jit(solution)/shard_map/psum | solution.py:294
  (117 other events, 1114.2 us)
Sparse Core Ops, SparseCore 0:
  10.1 78.9 all-gather.5
  90.7 169.1 all-gather.7
  417.3 25.5 reduce-scatter.8
  445.1 75.2 reduce-scatter.6
  522.5 77.3 reduce-scatter.10
  644.1 71.1 all-reduce.8
  717.6 64.7 reduce-scatter.12
  794.0 45.9 all-reduce.6
where the time goes:
time: 858 us; the launch traced here: 850 us
  local copies, waits for them, and re-layouts  199 us (23%)
  other arithmetic  185 us (22%)
  matrix products  163 us (19%)
  waiting for transfers between devices  147 us (17%)
  blocking collectives  89.4 us (10%)
  starting transfers between devices  49 us (6%)
  between operations  17 us (2%)
    unnamed x233, local copies, waits for them, and re-layouts  53.9 us
    psum x1, waiting for transfers between devices, body(): early_summed = lax.psum(early_shards, 'ctx')  47.9 us
    unnamed x1, blocking collectives  33.7 us
    ppermute x12, waiting for transfers between devices, group_return(): back.append(lax.ppermute(parts[shift], 'ctx', pairs))  30.5 us
    convert_element_type x1, other arithmetic, body(): d_scores = (probs * (d_probs - row_delta)).astype(jnp.bfloat16)  23.8 us
    psum x1, waiting for transfers between devices, body(): qkv_summed = lax.psum(qkv_shard, 'ctx')  23.3 us
    all_gather x1, blocking collectives, body(): d_mod_all = lax.all_gather(d_mod, 'shard', axis=0, tiled=True)  21.6 us
    ppermute x12, waiting for transfers between devices, group_send(): block = lax.ppermute(block, 'ctx', pairs)  19.6 us
  transfers between devices with their start and end apart: 44, of which 18 were waited for; matrix products, arithmetic and copies ran while one was open for 53% of the time, Pallas kernels for 0%

commit v1 on v0

--- a/solution.py
+++ b/solution.py
@@ -2,6 +2,29 @@
 import jax.numpy as jnp
 from jax import lax
 from jax.sharding import PartitionSpec as P
+
+
+def _pass_series(vector):
+    long_array, aux, placed = (lax.axis_size("shard"), lax.axis_index("shard"), vector.shape[0])
+    buffers = []
+    for b, no in enumerate(vector.shape):
+        buffers.append(no * long_array if b == 0 else no)
+    plain = lax.dynamic_update_slice_in_dim(
+        jnp.zeros(buffers, vector.dtype), vector, aux * placed, axis=0
+    )
+    w = 1
+    while w < long_array:
+        chunks = []
+        b = 0
+        while b < long_array:
+            chunks.append((b, (b + 1) % long_array))
+            b = b + 1
+        vector = lax.ppermute(vector, axis_name="shard", perm=chunks)
+        plain = lax.dynamic_update_slice_in_dim(
+            plain, vector, (aux - w) % long_array * placed, axis=0
+        )
+        w += 1
+    return plain
 
 
 def layer_norm(values):
@@ -274,7 +297,7 @@
         [d_gamma_one, d_gamma_two, d_scale_one, d_scale_two, d_shift_one, d_shift_two], axis=1
     )
     d_mod = lax.psum(d_mod_part, "ctx").astype(jnp.bfloat16).reshape(map_count, 6 * model_width)
-    d_mod_all = lax.all_gather(d_mod, "shard", axis=0, tiled=True)
+    d_mod_all = _pass_series(d_mod)
     g_ada = jnp.einsum(
         "md,mc->dc", cond_cols, d_mod_all, preferred_element_type=jnp.float32
     ).reshape(ada_rows, 6, model_width)

time: 858 us -> 860 us (level)
  blocking collectives: 89.4 us -> 67.6 us
  starting transfers between devices: 49 us -> 61.4 us
    all_gather x1 -> x0, blocking collectives: 21.6 us -> none  [body(): d_mod_all = lax.all_gather(d_mod, 'shard', axis=0, tiled=True)]
    ppermute x0 -> x3, starting transfers between devices: none -> 11.8 us  [_pass_series(): vector = lax.ppermute(vector, axis_name='shard', perm=chunks)]
    unnamed x233 -> x232, local copies, waits for them, and re-layouts: 53.9 us -> 53.7 us
  transfers between devices with their start and end apart: 44 -> 47, of which waited for: 18 -> 21; matrix products, arithmetic and copies ran while one was open for 53% -> 53% of each run, Pallas kernels for 0% -> 0%
where the time goes in v1:
time: 860 us; the launch traced here: 852 us
  local copies, waits for them, and re-layouts  202 us (23%)
  other arithmetic  185 us (22%)
  matrix products  163 us (19%)
  waiting for transfers between devices  155 us (18%)
  blocking collectives  67.6 us (8%)
  starting transfers between devices  61.4 us (7%)
  between operations  17.1 us (2%)
    unnamed x232, local copies, waits for them, and re-layouts  53.7 us
    psum x1, waiting for transfers between devices, body(): early_summed = lax.psum(early_shards, 'ctx')  47.9 us
    unnamed x1, blocking collectives  33.7 us
    ppermute x12, waiting for transfers between devices, group_return(): back.append(lax.ppermute(parts[shift], 'ctx', pairs))  30.5 us
    psum x1, waiting for transfers between devices, body(): qkv_summed = lax.psum(qkv_shard, 'ctx')  25.4 us
    convert_element_type x1, other arithmetic, body(): d_scores = (probs * (d_probs - row_delta)).astype(jnp.bfloat16)  23.8 us
    ppermute x12, waiting for transfers between devices, group_send(): block = lax.ppermute(block, 'ctx', pairs)  19.5 us
    all_gather x1, waiting for transfers between devices, body(): packed_all = lax.all_gather(packed, 'shard', axis=0, tiled=False)  18.9 us
  transfers between devices with their start and end apart: 47, of which 21 were waited for; matrix products, arithmetic and copies ran while one was open for 53% of the time, Pallas kernels for 0%

profile of v1, /device:TPU:0, one launch (start us, length us, event | category | flops | bytes accessed | tf_op | source)
XLA Modules:
  0.0 851.8 jit_solution(3133075433952976300)
XLA Ops:
  9.6 15.1 %all-gather.1 = bf16[4,6,1024]{2,1,0:T(8,128)(2,1)S(1)} all-gather(bf16[1,6,1024]{2,1,0:T(8,128)(2,1)} %bitcast.398), channel_id=1, replica_groups=mesh['shard'=4,'ctx'=4,'tp'=2] {'shard'}, dimensions={0}, use_global_device_ids=true | all-gather | bytes 61440 | tf_op jit(solution)/shard_map/all_gather | solution.py:168
  29.9 33.7 %fusion = f32[8,6144]{1,0:T(8,128)S(1)} fusion(f32[24,6144]{1,0:T(8,128)} %fusion.65), kind=kCustom, calls=%all-reduce-scatter | all-reduce-scatter fusion | flops 196609 | bytes 786944
  71.8 10.8 %pad_maximum_fusion = bf16[1179648]{0:T(1024)(128)(2,1)} fusion(bf16[524288]{0:T(1024)(128)(2,1)S(1)} %bitcast.365, bf16[524288]{0:T(1024)(128)(2,1)S(1)} %bitcast.364, bf16[131072]{0:T(1024)(128)(2,1)S(1)} %bitcast.375), kind=kLoop, calls=%fused_computation.87 | loop fusion | flops 7077888 | bytes 4718592 | tf_op jit(solution)/shard_map/concatenate | solution.py:153
  153.9 17.3 %select_reduce_fusion = (f32[6,2,4,170]{3,2,1,0:T(4,128)S(1)}, f32[6,2,4,170,4,170]{3,5,4,2,1,0:T(8,128)}) fusion(pred[6,4,170,4,170]{2,4,3,1,0:T(8,128)(4,1)} %broadcast_compare_fusion, bf16[1,6,170,2,64]{2,4,0,3,1:T(8,128)(2,1)} %bitcast.37, bf16[1,6,170,2,64]{2,4,0,3,1:T(8,128)(2,1)} %bitcast.35, bf16[1,6,170,2,64]{2,4,0,3,1:T(8,128)(2,1)} %bitcast.33, ...), kind=kOutput, calls=%fused_computation.12 | convolution fusion | flops 729691648 | bytes 27091200 | tf_op jit(solution)/shard_map/amqgd,bmkgd->mgaqbk/dot_general | solution.py:207
  171.2 15.7 %fusion.3 = f32[6,2,4,170]{3,2,1,0:T(4,128)S(1)} fusion(f32[6,2,4,170,4,170]{3,5,4,2,1,0:T(8,128)} %get-tuple-element.186, f32[6,2,4,170]{3,2,1,0:T(4,128)S(1)} %get-tuple-element.185, pred[6,4,170,4,170]{2,4,3,1,0:T(8,128)(4,1)} %broadcast_compare_fusion), kind=kLoop, calls=%fused_computation.13 | loop fusion | flops 16638240 | bytes 25034880 | tf_op jit(solution)/shard_map/reduce_sum | solution.py:215
  193.7 12.2 %divide_convert_fusion = bf16[6,2,4,170,4,170]{3,5,4,2,1,0:T(8,128)(2,1)} fusion(f32[6,2,4,170,4,170]{3,5,4,2,1,0:T(8,128)S(1)} %copy-done, f32[6,2,4,170]{3,2,1,0:T(4,128)S(1)} %fusion.3, f32[6,2,4,170]{3,2,1,0:T(4,128)S(1)} %get-tuple-element.185, pred[6,4,170,4,170]{2,4,3,1,0:T(8,128)(4,1)} %broadcast_compare_fusion), kind=kLoop, calls=%fused_computation.10 | loop fusion | flops 22195200 | bytes 36132480 | tf_op jit(solution)/shard_map/convert_element_type | solution.py:217
  205.9 9.6 %fusion.35 = bf16[4,6,170,2,64]{2,4,0,3,1:T(8,128)(2,1)S(1)} fusion(bf16[6,2,4,170,4,170]{3,5,4,2,1,0:T(8,128)(2,1)} %divide_convert_fusion, bf16[1,6,170,2,64]{2,4,0,3,1:T(8,128)(2,1)} %bitcast.15, bf16[1,6,170,2,64]{2,4,0,3,1:T(8,128)(2,1)} %bitcast.13, bf16[1,6,170,2,64]{2,4,0,3,1:T(8,128)(2,1)} %bitcast.11, ...), kind=kOutput, calls=%fused_computation.107 | convolution fusion | flops 714946560 | bytes 13186560 | tf_op jit(solution)/shard_map/mgaqbk,bmkgd->amqgd/dot_general | solution.py:218
  241.0 18.9 %all-gather.7.cloned.1.call-done = bf16[4718592]{0:T(1024)(128)(2,1)} async-done(((bf16[1179648]{0:T(1024)(128)(2,1)}), bf16[4718592]{0:T(1024)(128)(2,1)}) %all-gather.7.cloned.1.call-update) | async-done | bytes 9437200 | tf_op jit(solution)/shard_map/all_gather | solution.py:156
  259.9 12.5 %reshape.660 = bf16[4,1179648]{1,0:T(4,128)(2,1)} reshape(bf16[4718592]{0:T(1024)(128)(2,1)} %all-gather.7.cloned.1.call-done) | data formatting | bytes 18874368 | tf_op jit(solution)/shard_map/all_gather | solution.py:156
  278.0 8.3 fusion.72
  286.3 8.0 reshape_reshape.7
  305.5 9.2 %multiply_reduce_fusion.6 = (f32[]{:T(128)}, f32[1020,1024]{1,0:T(8,128)}) fusion(f32[1020,1024]{1,0:T(8,128)} %mul.544, f32[1024]{0:T(1024)S(1)} %copy-done.76, f32[1020,1024]{1,0:T(8,128)} %fusion.76, f32[1020,1024]{1,0:T(8,128)} %collective-permute-done.12), kind=kLoop, calls=%fused_computation.58 | loop fusion | flops 5222399 | bytes 16715780 | tf_op jit(solution)/shard_map/reduce_sum | solution.py:325
  327.9 7.5 fusion.77
  335.4 10.6 %fusion.69 = (f32[2048]{0:T(1024)}, bf16[1020,2048]{1,0:T(8,128)(2,1)S(1)}) fusion(f32[1020,2048]{1,0:T(8,128)S(1)} %fusion.77, f32[2048]{0:T(1024)S(1)} %copy-done.97, bf16[1020,1024]{1,0:T(8,128)(2,1)S(1)} %copy-done.30, bf16[2048,1024]{0,1:T(8,128)(2,1)S(1)} %bitcast.360), kind=kOutput, calls=%fused_computation.245 | convolution fusion | flops 4324145152 | bytes 18833408 | tf_op jit(solution)/shard_map/rd,fd->rf/dot_general | solution.py:241
  352.7 6.9 fusion.67
  366.3 6.8 add.471
  377.4 9.3 %multiply_reduce_fusion.5 = (f32[]{:T(128)}, f32[1020,1024]{1,0:T(8,128)}) fusion(f32[1020,1024]{1,0:T(8,128)} %mul.547, f32[1024]{0:T(1024)S(1)} %copy-done.85, f32[1020,1024]{1,0:T(8,128)} %fusion.67, f32[1020,1024]{1,0:T(8,128)} %collective-permute-done.13), kind=kLoop, calls=%fused_computation.57 | loop fusion | flops 5222399 | bytes 16715780 | tf_op jit(solution)/shard_map/reduce_sum | solution.py:325
  390.9 8.3 multiply_reduce_fusion
  417.1 8.3 convolution_convert_fusion.1
  442.6 11.9 %convolution_convert_fusion = bf16[2048,1024]{1,0:T(8,128)(2,1)} fusion(bf16[1020,1024]{1,0:T(8,128)(2,1)S(1)} %copy-done.31, f32[1020,2048]{1,0:T(8,128)} %copy-done.102, f32[2048]{0:T(1024)S(1)} %copy-done.98), kind=kOutput, calls=%fused_computation.65 | convolution fusion | flops 4301176832 | bytes 14647296 | tf_op jit(solution)/shard_map/rf,rd->fd/dot_general | solution.py:240
  459.8 11.7 %fusion.38 = bf16[4,6,170,2,64]{2,4,0,3,1:T(8,128)(2,1)S(1)} fusion(bf16[6,2,4,170,4,170]{3,5,4,2,1,0:T(8,128)(2,1)} %divide_convert_fusion, bf16[1,6,170,2,64]{2,4,0,3,1:T(8,128)(2,1)} %bitcast.373, bf16[1,6,170,2,64]{2,4,0,3,1:T(8,128)(2,1)S(1)} %bitcast.371, bf16[1,6,170,2,64]{2,4,0,3,1:T(8,128)(2,1)S(1)} %bitcast.369, ...), kind=kOutput, calls=%fused_computation.110 | convolution fusion | flops 714946560 | bytes 13186560 | tf_op jit(solution)/shard_map/mgaqbk,amqgd->bmkgd/dot_general | solution.py:271
  471.6 18.3 %fusion.1 = (f32[6,2,4,170]{3,2,1,0:T(4,128)S(1)}, f32[6,2,4,170,4,170]{3,5,4,2,1,0:T(8,128)}) fusion(bf16[6,2,4,170,4,170]{3,5,4,2,1,0:T(8,128)(2,1)} %divide_convert_fusion, bf16[1,6,170,2,64]{2,4,0,3,1:T(8,128)(2,1)} %bitcast.15, bf16[1,6,170,2,64]{2,4,0,3,1:T(8,128)(2,1)} %bitcast.13, bf16[1,6,170,2,64]{2,4,0,3,1:T(8,128)(2,1)} %bitcast.11, ...), kind=kOutput, calls=%fused_computation.8 | convolution fusion | flops 735240448 | bytes 35414400 | tf_op jit(solution)/shard_map/amqgd,bmkgd->mgaqbk/dot_general | solution.py:259
  494.4 23.8 %fusion.2 = bf16[6,2,4,170,4,170]{3,5,4,2,1,0:T(8,128)(2,1)S(1)} fusion(f32[6,2,4,170,4,170]{3,5,4,2,1,0:T(8,128)} %get-tuple-element.188, f32[6,2,4,170]{3,2,1,0:T(4,128)S(1)} %get-tuple-element.187, f32[6,2,4,170]{3,2,1,0:T(4,128)S(1)} %copy-done.55, f32[6,2,4,170]{3,2,1,0:T(4,128)S(1)} %copy-done.53, f32[6,2,4,170,4,170]{3,5,4,2,1,0:T(8,128)} %get-tuple-element.186, ...), kind=kLoop, calls=%fused_computation.9 | loop fusion | flops 44390400 | bytes 58360320 | tf_op jit(solution)/shard_map/convert_element_type | solution.py:263
  528.6 12.4 %fusion.37 = bf16[4,6,170,2,64]{2,4,0,3,1:T(8,128)(2,1)S(1)} fusion(bf16[6,2,4,170,4,170]{3,5,4,2,1,0:T(8,128)(2,1)} %copy-done.1, bf16[1,6,170,2,64]{2,4,0,3,1:T(8,128)(2,1)} %bitcast.388, bf16[1,6,170,2,64]{2,4,0,3,1:T(8,128)(2,1)} %bitcast.390, bf16[1,6,170,2,64]{2,4,0,3,1:T(8,128)(2,1)} %bitcast.392, bf16[1,6,170,2,64]{2,4,0,3,1:T(8,128)(2,1)} %get-tuple-element.162), kind=kOutput, calls=%fused_computation.109 | convolution fusion | flops 714946560 | bytes 13186560 | tf_op jit(solution)/shard_map/mgaqbk,amqgd->bmkgd/dot_general | solution.py:268
  556.4 7.3 collective-permute-done.23
  571.7 7.1 collective-permute-done.20
  634.7 9.1 %add_add_fusion.4 = (bf16[6,170,1,512]{3,1,2,0:T(8,128)(2,1)}, bf16[6,170,1,512]{3,1,2,0:T(8,128)(2,1)}) fusion(f32[6,170,1,512]{3,1,2,0:T(8,128)} %copy.255, f32[6,170,1,512]{3,1,2,0:T(8,128)} %copy.253, f32[6,170,1,512]{3,1,2,0:T(8,128)S(1)} %copy-done.18, f32[512]{0:T(512)S(1)} %copy-done.80, f32[512]{0:T(512)S(1)} %mul.506, ...), kind=kLoop, calls=%fused_computation.68 | loop fusion | flops 6266880 | bytes 18804736 | tf_op jit(solution)/shard_map/transpose(jvp())/add_any | solution.py:41
  654.3 7.0 fusion.78
  667.2 47.9 %all-reduce.9.cloned.1.call-done = (bf16[256,2048]{1,0:T(8,128)(2,1)}, bf16[512,256]{1,0:T(8,128)(2,1)}, bf16[2048,256]{1,0:T(8,128)(2,1)}) async-done(((bf16[256,2048]{1,0:T(8,128)(2,1)}, bf16[512,256]{1,0:T(8,128)(2,1)}, bf16[2048,256]{1,0:T(8,128)(2,1)}), (bf16[256,2048]{1,0:T(8,128)(2,1)}, bf16[512,256]{1,0:T(8,128)(2,1)}, bf16[2048,256]{1,0:T(8,128)(2,1)})) %all-reduce.9.cloned.1.call-update) | async-done | bytes 2359312 | tf_op jit(solution)/shard_map/psum | solution.py:314
  728.6 6.9 add.475
  745.8 18.8 %all-reduce.10 = bf16[6,6,1024]{2,1,0:T(8,128)(2,1)S(1)} all-reduce(f32[6,6,1024]{2,1,0:T(8,128)S(1)} %stack.200), channel_id=1, replica_groups=mesh['shard'=4,'ctx'=4,'tp'=2] {'ctx'}, use_global_device_ids=true, to_apply=%region_24.26 | all-reduce | flops 36864 | bytes 221184 | tf_op jit(solution)/shard_map/psum | solution.py:299
  816.6 25.4 %all-reduce.7.cloned.1.call-done = bf16[256,3,512]{2,0,1:T(8,128)(2,1)} async-done(((bf16[256,3,512]{2,0,1:T(8,128)(2,1)}), bf16[256,3,512]{2,0,1:T(8,128)(2,1)}) %all-reduce.7.cloned.1.call-update) | async-done | bytes 786448 | tf_op jit(solution)/shard_map/psum | solution.py:317
  (503 shorter events, 397.9 us)
Async XLA Ops:
  7.2 90.3 %all-gather.5.cloned.1.call-start = ((), (), s32[]{:S(2)}) async-start(), calls=%async_computation.5 | async-start | bytes 3932160 | tf_op jit(solution)/shard_map/all_gather | solution.py:152
  9.5 250.4 %all-gather.7.cloned.1.call-start = ((), (), s32[]{:S(2)}) async-start(), calls=%async_computation.11 | async-start | bytes 11796480 | tf_op jit(solution)/shard_map/all_gather | solution.py:156
  63.6 29.0 %collective-permute-start.37 = (f32[6,6144]{1,0:T(8,128)S(1)}, f32[6,6144]{1,0:T(8,128)}, u32[]{:S(2)}, u32[]{:S(2)}) collective-permute-start(f32[6,6144]{1,0:T(8,128)S(1)} %slice.187), channel_id=1, source_target_pairs={{0,8},{8,16},{16,24},{1,9},{9,17},{17,25},{2,10},{10,18},{18,26},{... | collective-permute-start | bytes 442376
  82.6 561.1 %reduce-scatter.9.cloned.1.call-start = ((), (), s32[]{:S(2)}) async-start(), calls=%async_computation.7 | async-start | bytes 1310720 | tf_op jit(solution)/shard_map/reduce_scatter | solution.py:311
  117.8 19.4 %collective-permute-start.7 = (bf16[6,170,2,64]{1,3,2,0:T(8,128)(2,1)}, bf16[6,170,2,64]{1,3,2,0:T(8,128)(2,1)}, u32[]{:S(2)}, u32[]{:S(2)}) collective-permute-start(bf16[6,170,2,64]{1,3,2,0:T(8,128)(2,1)} %get-tuple-element.168), channel_id=1, source_target_pairs={{0,4},{2,6},{4,0},{6,2},{1,5},{3,7},{5,1},{7,3},{8,12},{10,14},{12... | collective-permute-start | bytes 783368 | tf_op jit(solution)/shard_map/ppermute | solution.py:86
  118.3 20.8 %collective-permute-start.6 = (bf16[6,170,2,64]{1,3,2,0:T(8,128)(2,1)}, bf16[6,170,2,64]{1,3,2,0:T(8,128)(2,1)}, u32[]{:S(2)}, u32[]{:S(2)}) collective-permute-start(bf16[6,170,2,64]{1,3,2,0:T(8,128)(2,1)} %get-tuple-element.169), channel_id=1, source_target_pairs={{0,2},{2,4},{4,6},{6,0},{1,3},{3,5},{5,7},{7,1},{8,10},{10,12},{12... | collective-permute-start | bytes 783368 | tf_op jit(solution)/shard_map/ppermute | solution.py:86
  124.6 19.9 %collective-permute-start.5 = (bf16[6,170,2,64]{1,3,2,0:T(8,128)(2,1)S(1)}, bf16[6,170,2,64]{1,3,2,0:T(8,128)(2,1)S(1)}, u32[]{:S(2)}, u32[]{:S(2)}) collective-permute-start(bf16[6,170,2,64]{1,3,2,0:T(8,128)(2,1)S(1)} %get-tuple-element.163), channel_id=1, source_target_pairs={{0,6},{2,0},{4,2},{6,4},{1,7},{3,1},{5,3},{7,5},{8,14},{10,8},{12,... | collective-permute-start | bytes 783368 | tf_op jit(solution)/shard_map/ppermute | solution.py:86
  126.9 25.8 %collective-permute-start.4 = (bf16[6,170,2,64]{1,3,2,0:T(8,128)(2,1)S(1)}, bf16[6,170,2,64]{1,3,2,0:T(8,128)(2,1)S(1)}, u32[]{:S(2)}, u32[]{:S(2)}) collective-permute-start(bf16[6,170,2,64]{1,3,2,0:T(8,128)(2,1)S(1)} %get-tuple-element.164), channel_id=1, source_target_pairs={{0,4},{2,6},{4,0},{6,2},{1,5},{3,7},{5,1},{7,3},{8,12},{10,14},{12... | collective-permute-start | bytes 783368 | tf_op jit(solution)/shard_map/ppermute | solution.py:86
  128.4 25.5 %collective-permute-start.3 = (bf16[6,170,2,64]{1,3,2,0:T(8,128)(2,1)S(1)}, bf16[6,170,2,64]{1,3,2,0:T(8,128)(2,1)S(1)}, u32[]{:S(2)}, u32[]{:S(2)}) collective-permute-start(bf16[6,170,2,64]{1,3,2,0:T(8,128)(2,1)S(1)} %get-tuple-element.165), channel_id=1, source_target_pairs={{0,2},{2,4},{4,6},{6,0},{1,3},{3,5},{5,7},{7,1},{8,10},{10,12},{12... | collective-permute-start | bytes 783368 | tf_op jit(solution)/shard_map/ppermute | solution.py:86
  137.2 68.7 %collective-permute-start.2 = (bf16[6,170,2,64]{1,3,2,0:T(8,128)(2,1)}, bf16[6,170,2,64]{1,3,2,0:T(8,128)(2,1)}, u32[]{:S(2)}, u32[]{:S(2)}) collective-permute-start(bf16[6,170,2,64]{1,3,2,0:T(8,128)(2,1)} %get-tuple-element.159), channel_id=1, source_target_pairs={{0,6},{2,0},{4,2},{6,4},{1,7},{3,1},{5,3},{7,5},{8,14},{10,8},{12,... | collective-permute-start | bytes 783368 | tf_op jit(solution)/shard_map/ppermute | solution.py:86
  139.0 66.8 %collective-permute-start.1 = (bf16[6,170,2,64]{1,3,2,0:T(8,128)(2,1)}, bf16[6,170,2,64]{1,3,2,0:T(8,128)(2,1)}, u32[]{:S(2)}, u32[]{:S(2)}) collective-permute-start(bf16[6,170,2,64]{1,3,2,0:T(8,128)(2,1)} %get-tuple-element.160), channel_id=1, source_target_pairs={{0,4},{2,6},{4,0},{6,2},{1,5},{3,7},{5,1},{7,3},{8,12},{10,14},{12... | collective-permute-start | bytes 783368 | tf_op jit(solution)/shard_map/ppermute | solution.py:86
  144.4 61.4 %collective-permute-start = (bf16[6,170,2,64]{1,3,2,0:T(8,128)(2,1)}, bf16[6,170,2,64]{1,3,2,0:T(8,128)(2,1)}, u32[]{:S(2)}, u32[]{:S(2)}) collective-permute-start(bf16[6,170,2,64]{1,3,2,0:T(8,128)(2,1)} %get-tuple-element.161), channel_id=1, source_target_pairs={{0,2},{2,4},{4,6},{6,0},{1,3},{3,5},{5,7},{7,1},{8,10},{10,12},{12... | collective-permute-start | bytes 783368 | tf_op jit(solution)/shard_map/ppermute | solution.py:86
  278.0 27.5 %collective-permute-start.12 = (f32[1020,1024]{1,0:T(8,128)}, f32[1020,1024]{1,0:T(8,128)}, u32[]{:S(2)}, u32[]{:S(2)}) collective-permute-start(f32[1020,1024]{1,0:T(8,128)} %fusion.76), channel_id=1, source_target_pairs={{0,1},{1,0},{2,3},{3,2},{4,5},{5,4},{6,7},{7,6},{8,9},{9,8},{10,11... | collective-permute-start | bytes 12533768 | tf_op jit(solution)/shard_map/ppermute | solution.py:57
  417.1 226.7 %reduce-scatter.7.cloned.1.call-start = ((), (), s32[]{:S(2)}) async-start(), calls=%async_computation.6 | async-start | bytes 5242880 | tf_op jit(solution)/shard_map/reduce_scatter | solution.py:310
  425.5 218.3 %reduce-scatter.11.cloned.1.call-start = ((), (), s32[]{:S(2)}) async-start(), calls=%async_computation.8 | async-start | bytes 5242880 | tf_op jit(solution)/shard_map/reduce_scatter | solution.py:312
  438.2 19.0 %collective-permute-start.15 = (bf16[6,170,2,64]{1,3,2,0:T(8,128)(2,1)S(1)}, bf16[6,170,2,64]{1,3,2,0:T(8,128)(2,1)S(1)}, u32[]{:S(2)}, u32[]{:S(2)}) collective-permute-start(bf16[6,170,2,64]{1,3,2,0:T(8,128)(2,1)S(1)} %bitcast.382), channel_id=1, source_target_pairs={{0,2},{2,4},{4,6},{6,0},{1,3},{3,5},{5,7},{7,1},{8,10},{10,12},{12... | collective-permute-start | bytes 783368 | tf_op jit(solution)/shard_map/ppermute | solution.py:86
  439.7 19.3 %collective-permute-start.16 = (bf16[6,170,2,64]{1,3,2,0:T(8,128)(2,1)S(1)}, bf16[6,170,2,64]{1,3,2,0:T(8,128)(2,1)S(1)}, u32[]{:S(2)}, u32[]{:S(2)}) collective-permute-start(bf16[6,170,2,64]{1,3,2,0:T(8,128)(2,1)S(1)} %bitcast.381), channel_id=1, source_target_pairs={{0,4},{2,6},{4,0},{6,2},{1,5},{3,7},{5,1},{7,3},{8,12},{10,14},{12... | collective-permute-start | bytes 783368 | tf_op jit(solution)/shard_map/ppermute | solution.py:86
  441.2 17.9 %collective-permute-start.17 = (bf16[6,170,2,64]{1,3,2,0:T(8,128)(2,1)S(1)}, bf16[6,170,2,64]{1,3,2,0:T(8,128)(2,1)S(1)}, u32[]{:S(2)}, u32[]{:S(2)}) collective-permute-start(bf16[6,170,2,64]{1,3,2,0:T(8,128)(2,1)S(1)} %bitcast.380), channel_id=1, source_target_pairs={{0,6},{2,0},{4,2},{6,4},{1,7},{3,1},{5,3},{7,5},{8,14},{10,8},{12,... | collective-permute-start | bytes 783368 | tf_op jit(solution)/shard_map/ppermute | solution.py:86
  454.5 260.6 %all-reduce.9.cloned.1.call-start = ((), (), s32[]{:S(2)}) async-start(), calls=%async_computation.12 | async-start | bytes 4718592 | tf_op jit(solution)/shard_map/psum | solution.py:314
  491.0 55.1 %collective-permute-start.24 = (bf16[6,170,2,64]{1,3,2,0:T(8,128)(2,1)}, bf16[6,170,2,64]{1,3,2,0:T(8,128)(2,1)}, u32[]{:S(2)}, u32[]{:S(2)}) collective-permute-start(bf16[6,170,2,64]{1,3,2,0:T(8,128)(2,1)} %get-tuple-element.151), channel_id=1, source_target_pairs={{0,6},{2,0},{4,2},{6,4},{1,7},{3,1},{5,3},{7,5},{8,14},{10,8},{12,... | collective-permute-start | bytes 783368 | tf_op jit(solution)/shard_map/ppermute | solution.py:97
  492.6 54.0 %collective-permute-start.26 = (bf16[6,170,2,64]{1,3,2,0:T(8,128)(2,1)}, bf16[6,170,2,64]{1,3,2,0:T(8,128)(2,1)}, u32[]{:S(2)}, u32[]{:S(2)}) collective-permute-start(bf16[6,170,2,64]{1,3,2,0:T(8,128)(2,1)} %get-tuple-element.152), channel_id=1, source_target_pairs={{0,2},{2,4},{4,6},{6,0},{1,3},{3,5},{5,7},{7,1},{8,10},{10,12},{12... | collective-permute-start | bytes 783368 | tf_op jit(solution)/shard_map/ppermute | solution.py:97
  493.0 56.5 %collective-permute-start.25 = (bf16[6,170,2,64]{1,3,2,0:T(8,128)(2,1)}, bf16[6,170,2,64]{1,3,2,0:T(8,128)(2,1)}, u32[]{:S(2)}, u32[]{:S(2)}) collective-permute-start(bf16[6,170,2,64]{1,3,2,0:T(8,128)(2,1)} %get-tuple-element.153), channel_id=1, source_target_pairs={{0,4},{2,6},{4,0},{6,2},{1,5},{3,7},{5,1},{7,3},{8,12},{10,14},{12... | collective-permute-start | bytes 783368 | tf_op jit(solution)/shard_map/ppermute | solution.py:97
  546.1 20.8 %collective-permute-start.22 = (bf16[6,170,2,64]{1,3,2,0:T(8,128)(2,1)}, bf16[6,170,2,64]{1,3,2,0:T(8,128)(2,1)}, u32[]{:S(2)}, u32[]{:S(2)}) collective-permute-start(bf16[6,170,2,64]{1,3,2,0:T(8,128)(2,1)} %get-tuple-element.149), channel_id=1, source_target_pairs={{0,4},{2,6},{4,0},{6,2},{1,5},{3,7},{5,1},{7,3},{8,12},{10,14},{12... | collective-permute-start | bytes 783368 | tf_op jit(solution)/shard_map/ppermute | solution.py:97
  546.7 25.0 %collective-permute-start.18 = (bf16[6,170,2,64]{1,3,2,0:T(8,128)(2,1)}, bf16[6,170,2,64]{1,3,2,0:T(8,128)(2,1)}, u32[]{:S(2)}, u32[]{:S(2)}) collective-permute-start(bf16[6,170,2,64]{1,3,2,0:T(8,128)(2,1)} %get-tuple-element.143), channel_id=1, source_target_pairs={{0,6},{2,0},{4,2},{6,4},{1,7},{3,1},{5,3},{7,5},{8,14},{10,8},{12,... | collective-permute-start | bytes 783368 | tf_op jit(solution)/shard_map/ppermute | solution.py:97
  549.5 29.3 %collective-permute-start.20 = (bf16[6,170,2,64]{1,3,2,0:T(8,128)(2,1)}, bf16[6,170,2,64]{1,3,2,0:T(8,128)(2,1)}, u32[]{:S(2)}, u32[]{:S(2)}) collective-permute-start(bf16[6,170,2,64]{1,3,2,0:T(8,128)(2,1)} %get-tuple-element.144), channel_id=1, source_target_pairs={{0,2},{2,4},{4,6},{6,0},{1,3},{3,5},{5,7},{7,1},{8,10},{10,12},{12... | collective-permute-start | bytes 783368 | tf_op jit(solution)/shard_map/ppermute | solution.py:97
  554.8 26.5 %collective-permute-start.19 = (bf16[6,170,2,64]{1,3,2,0:T(8,128)(2,1)}, bf16[6,170,2,64]{1,3,2,0:T(8,128)(2,1)}, u32[]{:S(2)}, u32[]{:S(2)}) collective-permute-start(bf16[6,170,2,64]{1,3,2,0:T(8,128)(2,1)} %get-tuple-element.145), channel_id=1, source_target_pairs={{0,4},{2,6},{4,0},{6,2},{1,5},{3,7},{5,1},{7,3},{8,12},{10,14},{12... | collective-permute-start | bytes 783368 | tf_op jit(solution)/shard_map/ppermute | solution.py:97
  610.7 55.6 %collective-permute-start.33 = (f32[5131]{0:T(1024)S(1)}, f32[5131]{0:T(1024)S(1)}, u32[]{:S(2)}, u32[]{:S(2)}) collective-permute-start(f32[5131]{0:T(1024)S(1)} %concatenate.7), channel_id=1, source_target_pairs={{0,6},{2,0},{4,2},{6,4},{1,7},{3,1},{5,3},{7,5},{8,14},{10,8},{12,... | collective-permute-start | bytes 61580 | tf_op jit(solution)/shard_map/ppermute | solution.py:109
  610.8 55.5 %collective-permute-start.32 = (f32[5131]{0:T(1024)S(1)}, f32[5131]{0:T(1024)S(1)}, u32[]{:S(2)}, u32[]{:S(2)}) collective-permute-start(f32[5131]{0:T(1024)S(1)} %concatenate.7), channel_id=1, source_target_pairs={{0,4},{2,6},{4,0},{6,2},{1,5},{3,7},{5,1},{7,3},{8,12},{10,14},{12... | collective-permute-start | bytes 61580 | tf_op jit(solution)/shard_map/ppermute | solution.py:109
  611.4 55.0 %collective-permute-start.31 = (f32[5131]{0:T(1024)S(1)}, f32[5131]{0:T(1024)S(1)}, u32[]{:S(2)}, u32[]{:S(2)}) collective-permute-start(f32[5131]{0:T(1024)S(1)} %concatenate.7), channel_id=1, source_target_pairs={{0,2},{2,4},{4,6},{6,0},{1,3},{3,5},{5,7},{7,1},{8,10},{10,12},{12... | collective-permute-start | bytes 61580 | tf_op jit(solution)/shard_map/ppermute | solution.py:109
  643.8 149.6 %reduce-scatter.13.cloned.1.call-start = ((), (), s32[]{:S(2)}) async-start(), calls=%async_computation.9 | async-start | bytes 3932160 | tf_op jit(solution)/shard_map/reduce_scatter | solution.py:316
  661.3 67.3 %collective-permute-start.27 = (f32[1020,1024]{1,0:T(8,128)}, f32[1020,1024]{1,0:T(8,128)}, u32[]{:S(2)}, u32[]{:S(2)}) collective-permute-start(f32[1020,1024]{1,0:T(8,128)} %fusion.78), channel_id=1, source_target_pairs={{0,1},{1,0},{2,3},{3,2},{4,5},{5,4},{6,7},{7,6},{8,9},{9,8},{10,11... | collective-permute-start | bytes 12533768 | tf_op jit(solution)/shard_map/ppermute | solution.py:57
  715.1 126.8 %all-reduce.7.cloned.1.call-start = ((), (), s32[]{:S(2)}) async-start(), calls=%async_computation.10 | async-start | bytes 1572864 | tf_op jit(solution)/shard_map/psum | solution.py:317
  (120 other events, 1142.4 us)
Sparse Core Ops, SparseCore 0:
  10.1 78.9 all-gather.4
  90.7 169.1 all-gather.6
  417.2 25.5 reduce-scatter.8
  445.0 75.2 reduce-scatter.6
  522.4 77.2 reduce-scatter.10
  643.9 71.1 all-reduce.8
  717.4 63.6 reduce-scatter.12
  793.5 48.4 all-reduce.6
